TPU v7x, 32 devices: a whole 2x2x4 slice. The times are simulated.
32 devices in a mesh: dp: 16 (over z, x, core), tensor: 2 (over y).
Axes of the slice: x: 2, y: 2, z: 4, core: 2. Of those that a mesh axis runs over, the one named last changes fastest.
Arguments:
- context: bfloat16 [4096, 4096], P('dp', 'tensor'), may hold values from -6 to 6
- w_out: bfloat16 [4096, 4096], P('tensor'), may hold values from -1 to 1
- teacher_input: bfloat16 [4096, 4096], P(('dp', 'tensor')), may hold values from -6 to 6
- teacher_gain: bfloat16 [4096], replicated, may hold values from 0.5 to 1.5
- layer_weights: float32 [2], replicated, may hold values from 0.3 to 1.5
- teacher_head: bfloat16 [4096, 4], replicated, may hold values from -16 to 16
- student_hidden: bfloat16 [4096, 3072], P(('dp', 'tensor')), may hold values from -6 to 6
- student_input: bfloat16 [4096, 768], P(('dp', 'tensor')), may hold values from -10 to 10
- down_weight: bfloat16 [3072, 768], P(('dp', 'tensor')), may hold values from -0.109375 to 0.109375
- student_gain: bfloat16 [768], replicated, may hold values from 0.5 to 1.5
- student_head: bfloat16 [768, 4], replicated, may hold values from -32 to 32
- labels: int32 [4096], P(('dp', 'tensor')), may hold values from 0 to 3
- lengths: int32 [8], replicated, may hold values from 64 to 512
Outputs:
- grad_down: float32 [3072, 768], P(('dp', 'tensor'))
- grad_head: float32 [768, 4], replicated
- loss: float32 [], replicated
All inputs are finite; a program needn't handle non-finite values.
Results may differ from a plain program's by a relative error of at most 0.0075.
Values may be sent and summed in bfloat16 or wider, within the bound.
No kernel may reach another device: no remote copies, remote signals or barrier semaphores. Data moves between devices by JAX's collectives and lax.ppermute only.
A program may use at most 128 MiB of HBM per device.

v0:
```python
import jax
import jax.numpy as jnp
from jax import lax
from jax.sharding import PartitionSpec as P

SEQ = 512
label_weight = 0.5
teacher_eps = 1e-05
student_eps = 1e-07


def norm_rows(values, gain_vec, epsilon):
    center = values - jnp.mean(values, axis=-1, keepdims=True)
    spread = jnp.mean(center * center, axis=-1, keepdims=True)
    inverse = lax.rsqrt(spread + epsilon)
    scaled = center * inverse
    return (scaled * gain_vec, scaled, inverse)


def folder(ordered, row_piece):
    return jnp.dot(ordered, row_piece, preferred_element_type=jnp.float32)


def local(
    context,
    w_out,
    teacher_input,
    teacher_gain,
    layer_weights,
    teacher_head,
    student_hidden,
    student_input,
    down_weight,
    student_gain,
    student_head,
    labels,
    lengths,
):
    tok_rows = teacher_input.shape[0]
    tensor_size = lax.axis_size("tensor")
    attention = lax.psum_scatter(
        jnp.dot(context, w_out, preferred_element_type=jnp.float32).astype(jnp.bfloat16),
        "tensor",
        scatter_dimension=0,
        tiled=True,
    ).astype(jnp.float32)
    residual = teacher_input.astype(jnp.float32)
    layer_out = norm_rows(residual + attention, teacher_gain.astype(jnp.float32), teacher_eps)[0]
    blended = (layer_weights[0] * residual + layer_weights[1] * layer_out).astype(jnp.bfloat16)
    teacher_logits = jnp.dot(blended, teacher_head, preferred_element_type=jnp.float32)
    teacher_logp = jax.nn.log_softmax(teacher_logits, axis=-1)
    teacher_prob = jnp.exp(teacher_logp)
    ffn_out = folder(
        student_hidden, lax.all_gather(down_weight, ("dp", "tensor"), axis=0, tiled=True)
    )
    student_scale = student_gain.astype(jnp.float32)
    normed, scaled, inverse = norm_rows(
        student_input.astype(jnp.float32) + ffn_out, student_scale, student_eps
    )
    features = normed.astype(jnp.bfloat16)
    student_logits = jnp.dot(features, student_head, preferred_element_type=jnp.float32)
    student_logp = jax.nn.log_softmax(student_logits, axis=-1)
    student_prob = jnp.exp(student_logp)
    first_token = (lax.axis_index("dp") * tensor_size + lax.axis_index("tensor")) * tok_rows
    positions = first_token + jnp.arange(tok_rows, dtype=jnp.int32)
    sentence = positions // SEQ
    matches = sentence[:, None] == jnp.arange(lengths.shape[0], dtype=jnp.int32)[None, :]
    lengths_tok = jnp.sum(jnp.where(matches, lengths[None, :], 0), axis=1)
    validity = (positions % SEQ < lengths_tok).astype(jnp.float32)
    onehot = (
        labels[:, None] == jnp.arange(teacher_logits.shape[1], dtype=jnp.int32)[None, :]
    ).astype(jnp.float32)
    token_loss = jnp.sum(
        teacher_prob * (teacher_logp - student_logp), axis=1
    ) - label_weight * jnp.sum(onehot * student_logp, axis=1)
    loss_part = jnp.sum(validity * token_loss)
    logit_grad = (
        validity[:, None]
        * ((1.0 + label_weight) * student_prob - teacher_prob - label_weight * onehot)
    ).astype(jnp.bfloat16)
    head_term = lax.dot_general(
        features, logit_grad, (((0,), (0,)), ((), ())), preferred_element_type=jnp.float32
    )
    norm_grad = (
        jnp.dot(logit_grad, student_head.T, preferred_element_type=jnp.float32) * student_scale
    )
    grad_out = (
        (
            norm_grad
            - jnp.mean(norm_grad, axis=-1, keepdims=True)
            - scaled * jnp.mean(norm_grad * scaled, axis=-1, keepdims=True)
        )
        * inverse
    ).astype(jnp.bfloat16)
    grad_down = lax.psum_scatter(
        lax.dot_general(
            student_hidden, grad_out, (((0,), (0,)), ((), ())), preferred_element_type=jnp.float32
        ),
        ("dp", "tensor"),
        scatter_dimension=0,
        tiled=True,
    )
    head_total, loss_total, count_total = lax.psum(
        (head_term, loss_part, jnp.sum(validity)), ("dp", "tensor")
    )
    return (grad_down, head_total, loss_total / count_total)


def solution(mesh):
    return jax.shard_map(
        local,
        mesh=mesh,
        in_specs=(
            P("dp", "tensor"),
            P("tensor", None),
            P(("dp", "tensor"), None),
            P(),
            P(),
            P(),
            P(("dp", "tensor"), None),
            P(("dp", "tensor"), None),
            P(("dp", "tensor"), None),
            P(),
            P(),
            P(("dp", "tensor")),
            P(),
        ),
        out_specs=(P(("dp", "tensor"), None), P(), P()),
        check_vma=False,
    )
```

profile of v0, /device:TPU:0, one launch (start us, length us, event | category | flops | bytes accessed | tf_op | source)
XLA Modules:
  0.0 268.8 jit_solution(7776146395088304549)
XLA Ops:
  8.0 0.0 copy-start
  8.0 0.0 reduce-scatter.5.cloned.1.call-start
  8.1 1.2 copy-done
  9.2 11.5 %convolution_convert_fusion = bf16[256,4096]{1,0:T(8,128)(2,1)} fusion(bf16[256,2048]{1,0:T(8,128)(2,1)S(1)} %copy-done, bf16[2048,4096]{1,0:T(8,128)(2,1)} %param.15), kind=kOutput, calls=%fused_computation.1 | convolution fusion | flops 4296015872 | bytes 19922944 | tf_op jit(solution)/shard_map/dot_general | solution.py:42
  20.7 0.0 copy-start.8
  20.7 0.0 copy-start.6
  20.7 0.0 copy-start.9
  20.7 0.0 copy-start.11
  20.7 0.0 copy-start.1
  20.7 0.0 reduce-scatter.5.cloned.1.call-update
  20.7 0.0 all-gather.2.cloned.1.call-start
  20.8 0.5 all-gather.2.cloned.1.call-update
  21.3 0.0 reduce-scatter.7.cloned.1.call-start
  21.4 0.0 copy-done.8
  21.4 0.0 copy-done.6
  21.4 0.0 copy-done.9
  21.4 0.6 fusion.13
  22.0 0.0 copy-done.11
  22.0 0.1 select_reduce_fusion
  22.1 0.0 copy-start.10
  22.1 33.5 %reduce-scatter.5.cloned.1.call-done = bf16[128,4096]{1,0:T(8,128)(2,1)} async-done(((bf16[256,4096]{1,0:T(8,128)(2,1)}), bf16[128,4096]{1,0:T(8,128)(2,1)}) %reduce-scatter.5.cloned.1.call-update) | async-done | bytes 1048592 | tf_op jit(solution)/shard_map/reduce_scatter | solution.py:41
  55.7 0.0 copy-done.1
  55.7 0.0 copy-start.2
  55.7 1.7 fusion.3
  57.3 0.0 copy-done.2
  57.3 0.5 multiply_reduce_fusion
  57.9 0.0 copy-done.10
  57.9 0.0 copy-start.3
  57.9 0.0 copy-start.4
  57.9 2.2 fusion.15
  60.1 0.0 copy-start.5
  60.1 0.0 copy-start.7
  60.1 46.4 %all-gather.2.cloned.1.call-done = bf16[3072,768]{1,0:T(8,128)(2,1)} async-done(((bf16[96,768]{1,0:T(8,128)(2,1)}), bf16[3072,768]{1,0:T(8,128)(2,1)}) %all-gather.2.cloned.1.call-update) | async-done | bytes 4718608 | tf_op jit(solution)/shard_map/all_gather | solution.py:54
  106.5 0.0 copy-done.3
  106.5 0.0 copy-done.4
  106.5 3.2 %fusion.14 = (f32[128]{0:T(128)S(1)}, f32[128,768]{1,0:T(8,128)S(1)}) fusion(bf16[128,3072]{1,0:T(8,128)(2,1)S(1)} %copy-done.3, bf16[3072,768]{1,0:T(8,128)(2,1)} %all-gather.2.cloned.1.call-done, bf16[128,768]{1,0:T(8,128)(2,1)S(1)} %copy-done.4), kind=kOutput, calls=%fused_computation.48 | convolution fusion | flops 604274560 | bytes 6095360 | tf_op jit(solution)/shard_map/dot_general | solution.py:21
  109.8 0.2 multiply_reduce_fusion.2
  110.0 0.1 multiply_convert_fusion.1
  110.1 0.0 copy-done.5
  110.1 0.1 fusion.16
  110.2 0.1 exponential_reduce_fusion.1
  110.3 0.0 copy-done.7
  110.4 0.6 convert_reduce_fusion
  111.0 0.4 fusion.11
  111.4 5.2 %convolution_bitcast_fusion = f32[3072,768]{0,1:T(8,128)} fusion(bf16[128,3072]{1,0:T(8,128)(2,1)S(1)} %copy-done.3, f32[128,768]{1,0:T(8,128)S(1)} %get-tuple-element.31, f32[128,768]{1,0:T(8,128)S(1)} %get-tuple-element.26, f32[128]{0:T(128)S(1)} %get-tuple-element.32, f32[128]{0:T(128)S(1)} %get-tuple-element.33, f32[128]{0:T(128)S(1)} %add_rsqrt_fusion.1, ...), kind=kOutput, calls=%fused_computation | convolution fusion | flops 604667904 | bytes 11012096 | tf_op jit(solution)/shard_map/dot_general | solution.py:96
  116.6 9.6 %copy.19 = f32[3072,768]{1,0:T(8,128)} copy(f32[3072,768]{0,1:T(8,128)} %convolution_bitcast_fusion) | data formatting | bytes 18874368
  126.3 0.0 reduce-scatter.7.cloned.1.call-update
  126.3 0.1 fusion.17
  126.4 39.3 %all-reduce = (f32[768,4]{0,1:T(4,128)}, f32[]{:T(128)}, f32[]{:T(128)}) all-reduce(f32[768,4]{0,1:T(4,128)S(1)} %fusion.17, f32[]{:T(128)} %get-tuple-element.18, f32[]{:T(128)} %get-tuple-element.17), channel_id=1, replica_groups=mesh['dp'=16,'tensor'=2] {'dp','tensor'}, use_global_device_ids=true, to_apply=%region_11.13 | all-reduce | flops 3074 | bytes 24592 | tf_op jit(solution)/shard_map/psum | solution.py:103
  167.0 93.2 %reduce-scatter.7.cloned.1.call-done = f32[96,768]{1,0:T(8,128)} async-done(((f32[3072,768]{1,0:T(8,128)}), f32[96,768]{1,0:T(8,128)}) %reduce-scatter.7.cloned.1.call-update) | async-done | bytes 294928
  (13 shorter events, 0.1 us)
Async XLA Ops:
  8.0 1.2 copy-start
  8.0 47.6 %reduce-scatter.5.cloned.1.call-start = ((), (), s32[]{:S(2)}) async-start(), calls=%async_computation.3 | async-start | bytes 3145728 | tf_op jit(solution)/shard_map/reduce_scatter | solution.py:41
  20.7 0.7 copy-start.8
  20.7 0.7 copy-start.6
  20.7 0.8 copy-start.9
  20.7 1.3 copy-start.11
  20.7 35.0 %copy-start.1 = (bf16[128,4096]{1,0:T(8,128)(2,1)S(1)}, bf16[128,4096]{1,0:T(8,128)(2,1)}, u32[]{:S(2)}) copy-start(bf16[128,4096]{1,0:T(8,128)(2,1)} %param.16) | copy-start | bytes 3145732
  20.7 85.8 %all-gather.2.cloned.1.call-start = ((), (), s32[]{:S(2)}) async-start(), calls=%async_computation.2 | async-start | bytes 4866048 | tf_op jit(solution)/shard_map/all_gather | solution.py:54
  21.3 238.9 %reduce-scatter.7.cloned.1.call-start = ((), (), s32[]{:S(2)}) async-start(), calls=%async_computation.4 | async-start | bytes 9732096
  22.1 35.8 %copy-start.10 = (bf16[4096,4]{0,1:T(4,128)(2,1)S(1)}, bf16[4096,4]{0,1:T(4,128)(2,1)}, u32[]{:S(2)}) copy-start(bf16[4096,4]{0,1:T(4,128)(2,1)} %param.19) | copy-start | bytes 98308
  55.7 1.7 copy-start.2
  57.9 48.6 %copy-start.3 = (bf16[128,3072]{1,0:T(8,128)(2,1)S(1)}, bf16[128,3072]{1,0:T(8,128)(2,1)}, u32[]{:S(2)}) copy-start(bf16[128,3072]{1,0:T(8,128)(2,1)} %param.20) | copy-start | bytes 2359300
  57.9 48.6 %copy-start.4 = (bf16[128,768]{1,0:T(8,128)(2,1)S(1)}, bf16[128,768]{1,0:T(8,128)(2,1)}, u32[]{:S(2)}) copy-start(bf16[128,768]{1,0:T(8,128)(2,1)} %param.21) | copy-start | bytes 589828
  60.1 50.0 %copy-start.5 = (bf16[768,4]{0,1:T(4,128)(2,1)S(1)}, bf16[768,4]{0,1:T(4,128)(2,1)}, u32[]{:S(2)}) copy-start(bf16[768,4]{0,1:T(4,128)(2,1)} %param.24) | copy-start | bytes 18436
  60.1 50.2 %copy-start.7 = (s32[128]{0:T(128)S(1)}, s32[128]{0:T(128)}, u32[]{:S(2)}) copy-start(s32[128]{0:T(128)} %param.25) | copy-start | bytes 1540
Sparse Core Ops, SparseCore 0:
  20.9 34.7 reduce-scatter.4
Sparse Core Ops, SparseCore 1:
  24.1 82.3 all-gather.1
  126.4 133.8 reduce-scatter.6
where the time goes:
time: 269 us
  waiting for transfers between devices  174 us (65%)
  blocking collectives  39.3 us (15%)
  matrix products  22.7 us (8%)
  between operations  18.1 us (7%)
  local copies, waits for them, and re-layouts  11.5 us (4%)
  other arithmetic  3.44 us (1%)
    unnamed x4, waiting for transfers between devices  93.8 us
    all_gather x1, waiting for transfers between devices, local(): lax.all_gather(down_weight, ('dp', 'tensor'), axis=0, tiled=True)  46.4 us
    psum x1, blocking collectives, local(): lax.psum((head_term, loss_part, jnp.sum(validity)), ('dp', 'tensor'))  39.3 us
    reduce_scatter x1, waiting for transfers between devices, local(): lax.psum_scatter(jnp.dot(context, w_out, preferred_element_type=jnp.float...  33.5 us
    dot_general x1, matrix products, local(): jnp.dot(context, w_out, preferred_element_type=jnp.float32)  11.5 us
    unnamed x25, local copies, waits for them, and re-layouts  10.9 us
  transfers between devices with their start and end apart: 3, of which 3 were waited for; matrix products, arithmetic and copies ran while one was open for 2% of the time, Pallas kernels for 0%

commit v1 on v0

--- a/solution.py
+++ b/solution.py
@@ -7,6 +7,12 @@
 label_weight = 0.5
 teacher_eps = 1e-05
 student_eps = 1e-07
+
+
+def unite_cube(point, named_axis, shard_axis):
+    val2 = lax.psum(point, axis_name=named_axis)
+    response = lax.psum(val2, shard_axis)
+    return response
 
 
 def norm_rows(values, gain_vec, epsilon):
@@ -100,8 +106,8 @@
         scatter_dimension=0,
         tiled=True,
     )
-    head_total, loss_total, count_total = lax.psum(
-        (head_term, loss_part, jnp.sum(validity)), ("dp", "tensor")
+    head_total, loss_total, count_total = unite_cube(
+        (head_term, loss_part, jnp.sum(validity)), "tensor", "dp"
     )
     return (grad_down, head_total, loss_total / count_total)
 

time: 269 us -> 269 us (level)
  waiting for transfers between devices: 174 us -> 145 us
  blocking collectives: 39.3 us -> 67.9 us
    unnamed x4, waiting for transfers between devices: 93.8 us -> 65.1 us
    psum x1 -> x2, blocking collectives: 39.3 us -> 67.9 us  [the longest x1 58.6 us: unite_cube(): response = lax.psum(val2, shard_axis)]
where the time goes in v1:
time: 269 us
  waiting for transfers between devices  145 us (54%)
  blocking collectives  67.9 us (25%)
  matrix products  22.7 us (8%)
  between operations  18.2 us (7%)
  local copies, waits for them, and re-layouts  11.5 us (4%)
  other arithmetic  3.41 us (1%)
    unnamed x4, waiting for transfers between devices  65.1 us
    psum x1, blocking collectives, unite_cube(): response = lax.psum(val2, shard_axis)  58.6 us
    all_gather x1, waiting for transfers between devices, local(): lax.all_gather(down_weight, ('dp', 'tensor'), axis=0, tiled=True)  46.4 us
    reduce_scatter x1, waiting for transfers between devices, local(): lax.psum_scatter(jnp.dot(context, w_out, preferred_element_type=jnp.float...  33.5 us
    dot_general x1, matrix products, local(): jnp.dot(context, w_out, preferred_element_type=jnp.float32)  11.5 us
    unnamed x25, local copies, waits for them, and re-layouts  10.9 us
    psum x1, blocking collectives, unite_cube(): val2 = lax.psum(point, axis_name=named_axis)  9.31 us
  transfers between devices with their start and end apart: 3, of which 3 were waited for; matrix products, arithmetic and copies ran while one was open for 2% of the time, Pallas kernels for 0%

profile of v1, /device:TPU:0, one launch (start us, length us, event | category | flops | bytes accessed | tf_op | source)
XLA Modules:
  0.0 268.8 jit_solution(11434386944062099820)
XLA Ops:
  8.0 0.0 copy-start
  8.0 0.0 reduce-scatter.5.cloned.1.call-start
  8.1 1.2 copy-done
  9.2 11.5 %convolution_convert_fusion = bf16[256,4096]{1,0:T(8,128)(2,1)} fusion(bf16[256,2048]{1,0:T(8,128)(2,1)S(1)} %copy-done, bf16[2048,4096]{1,0:T(8,128)(2,1)} %param.15), kind=kOutput, calls=%fused_computation.1 | convolution fusion | flops 4296015872 | bytes 19922944 | tf_op jit(solution)/shard_map/dot_general | solution.py:48
  20.7 0.0 copy-start.8
  20.7 0.0 copy-start.6
  20.7 0.0 copy-start.9
  20.7 0.0 copy-start.11
  20.7 0.0 copy-start.1
  20.7 0.0 reduce-scatter.5.cloned.1.call-update
  20.7 0.0 all-gather.2.cloned.1.call-start
  20.8 0.5 all-gather.2.cloned.1.call-update
  21.3 0.0 reduce-scatter.7.cloned.1.call-start
  21.4 0.0 copy-done.8
  21.4 0.0 copy-done.6
  21.4 0.0 copy-done.9
  21.4 0.6 fusion.13
  22.0 0.0 copy-done.11
  22.0 0.1 select_reduce_fusion
  22.1 0.0 copy-start.10
  22.1 33.5 %reduce-scatter.5.cloned.1.call-done = bf16[128,4096]{1,0:T(8,128)(2,1)} async-done(((bf16[256,4096]{1,0:T(8,128)(2,1)}), bf16[128,4096]{1,0:T(8,128)(2,1)}) %reduce-scatter.5.cloned.1.call-update) | async-done | bytes 1048592 | tf_op jit(solution)/shard_map/reduce_scatter | solution.py:47
  55.7 0.0 copy-done.1
  55.7 0.0 copy-start.2
  55.7 1.7 fusion.3
  57.3 0.0 copy-done.2
  57.3 0.5 multiply_reduce_fusion
  57.9 0.0 copy-done.10
  57.9 0.0 copy-start.3
  57.9 0.0 copy-start.4
  57.9 2.2 fusion.15
  60.1 0.0 copy-start.5
  60.1 0.0 copy-start.7
  60.1 46.4 %all-gather.2.cloned.1.call-done = bf16[3072,768]{1,0:T(8,128)(2,1)} async-done(((bf16[96,768]{1,0:T(8,128)(2,1)}), bf16[3072,768]{1,0:T(8,128)(2,1)}) %all-gather.2.cloned.1.call-update) | async-done | bytes 4718608 | tf_op jit(solution)/shard_map/all_gather | solution.py:60
  106.5 0.0 copy-done.3
  106.5 0.0 copy-done.4
  106.5 3.2 %fusion.14 = (f32[128]{0:T(128)S(1)}, f32[128,768]{1,0:T(8,128)S(1)}) fusion(bf16[128,3072]{1,0:T(8,128)(2,1)S(1)} %copy-done.3, bf16[3072,768]{1,0:T(8,128)(2,1)} %all-gather.2.cloned.1.call-done, bf16[128,768]{1,0:T(8,128)(2,1)S(1)} %copy-done.4), kind=kOutput, calls=%fused_computation.48 | convolution fusion | flops 604274560 | bytes 6095360 | tf_op jit(solution)/shard_map/dot_general | solution.py:27
  109.8 0.2 multiply_reduce_fusion.2
  110.0 0.1 multiply_convert_fusion.1
  110.1 0.0 copy-done.5
  110.1 0.1 fusion.16
  110.2 0.1 exponential_reduce_fusion.1
  110.3 0.0 copy-done.7
  110.4 0.6 convert_reduce_fusion
  111.0 0.4 fusion.11
  111.4 5.2 %convolution_bitcast_fusion = f32[3072,768]{0,1:T(8,128)} fusion(bf16[128,3072]{1,0:T(8,128)(2,1)S(1)} %copy-done.3, f32[128,768]{1,0:T(8,128)S(1)} %get-tuple-element.34, f32[128,768]{1,0:T(8,128)S(1)} %get-tuple-element.29, f32[128]{0:T(128)S(1)} %get-tuple-element.35, f32[128]{0:T(128)S(1)} %get-tuple-element.36, f32[128]{0:T(128)S(1)} %add_rsqrt_fusion.1, ...), kind=kOutput, calls=%fused_computation | convolution fusion | flops 604667904 | bytes 11012096 | tf_op jit(solution)/shard_map/dot_general | solution.py:102
  116.6 9.6 %copy.19 = f32[3072,768]{1,0:T(8,128)} copy(f32[3072,768]{0,1:T(8,128)} %convolution_bitcast_fusion) | data formatting | bytes 18874368
  126.2 0.0 reduce-scatter.7.cloned.1.call-update
  126.2 0.1 fusion.17
  126.4 9.3 %all-reduce.1 = (f32[768,4]{0,1:T(4,128)S(1)}, f32[]{:T(128)}, f32[]{:T(128)}) all-reduce(f32[768,4]{0,1:T(4,128)S(1)} %fusion.17, f32[]{:T(128)} %get-tuple-element.18, f32[]{:T(128)} %get-tuple-element.17), channel_id=1, replica_groups=mesh['dp'=16,'tensor'=2] {'tensor'}, use_global_device_ids=true, to_apply=%region_11.13 | all-reduce | flops 3074 | bytes 24592 | tf_op jit(solution)/shard_map/psum | solution.py:13
  135.7 58.6 %all-reduce = (f32[768,4]{0,1:T(4,128)}, f32[]{:T(128)}, f32[]{:T(128)}) all-reduce(f32[768,4]{0,1:T(4,128)S(1)} %get-tuple-element.22, f32[]{:T(128)} %get-tuple-element.23, f32[]{:T(128)} %get-tuple-element.24), channel_id=1, replica_groups=mesh['dp'=16,'tensor'=2] {'dp'}, use_global_device_ids=true, to_apply=%region_12.14 | all-reduce | flops 3074 | bytes 24592 | tf_op jit(solution)/shard_map/psum | solution.py:14
  195.7 64.6 %reduce-scatter.7.cloned.1.call-done = f32[96,768]{1,0:T(8,128)} async-done(((f32[3072,768]{1,0:T(8,128)}), f32[96,768]{1,0:T(8,128)}) %reduce-scatter.7.cloned.1.call-update) | async-done | bytes 294928
  (13 shorter events, 0.1 us)
Async XLA Ops:
  8.0 1.2 copy-start
  8.0 47.6 %reduce-scatter.5.cloned.1.call-start = ((), (), s32[]{:S(2)}) async-start(), calls=%async_computation.3 | async-start | bytes 3145728 | tf_op jit(solution)/shard_map/reduce_scatter | solution.py:47
  20.7 0.7 copy-start.8
  20.7 0.7 copy-start.6
  20.7 0.8 copy-start.9
  20.7 1.3 copy-start.11
  20.7 35.0 %copy-start.1 = (bf16[128,4096]{1,0:T(8,128)(2,1)S(1)}, bf16[128,4096]{1,0:T(8,128)(2,1)}, u32[]{:S(2)}) copy-start(bf16[128,4096]{1,0:T(8,128)(2,1)} %param.16) | copy-start | bytes 3145732
  20.7 85.8 %all-gather.2.cloned.1.call-start = ((), (), s32[]{:S(2)}) async-start(), calls=%async_computation.2 | async-start | bytes 4866048 | tf_op jit(solution)/shard_map/all_gather | solution.py:60
  21.3 238.9 %reduce-scatter.7.cloned.1.call-start = ((), (), s32[]{:S(2)}) async-start(), calls=%async_computation.4 | async-start | bytes 9732096
  22.1 35.8 %copy-start.10 = (bf16[4096,4]{0,1:T(4,128)(2,1)S(1)}, bf16[4096,4]{0,1:T(4,128)(2,1)}, u32[]{:S(2)}) copy-start(bf16[4096,4]{0,1:T(4,128)(2,1)} %param.19) | copy-start | bytes 98308
  55.7 1.7 copy-start.2
  57.9 48.6 %copy-start.3 = (bf16[128,3072]{1,0:T(8,128)(2,1)S(1)}, bf16[128,3072]{1,0:T(8,128)(2,1)}, u32[]{:S(2)}) copy-start(bf16[128,3072]{1,0:T(8,128)(2,1)} %param.20) | copy-start | bytes 2359300
  57.9 48.6 %copy-start.4 = (bf16[128,768]{1,0:T(8,128)(2,1)S(1)}, bf16[128,768]{1,0:T(8,128)(2,1)}, u32[]{:S(2)}) copy-start(bf16[128,768]{1,0:T(8,128)(2,1)} %param.21) | copy-start | bytes 589828
  60.1 50.0 %copy-start.5 = (bf16[768,4]{0,1:T(4,128)(2,1)S(1)}, bf16[768,4]{0,1:T(4,128)(2,1)}, u32[]{:S(2)}) copy-start(bf16[768,4]{0,1:T(4,128)(2,1)} %param.24) | copy-start | bytes 18436
  60.1 50.2 %copy-start.7 = (s32[128]{0:T(128)S(1)}, s32[128]{0:T(128)}, u32[]{:S(2)}) copy-start(s32[128]{0:T(128)} %param.25) | copy-start | bytes 1540
Sparse Core Ops, SparseCore 0:
  20.9 34.7 reduce-scatter.4
Sparse Core Ops, SparseCore 1:
  24.1 82.3 all-gather.1
  126.3 133.9 reduce-scatter.6
